TPU v7x, 512 devices: a whole 4x4x16 slice. The times are simulated.
512 devices in a mesh: ingest: 8 (over y, core), owner: 64 (over x, z).
Axes of the slice: x: 4, y: 4, z: 16, core: 2. Of those that a mesh axis runs over, the one named last changes fastest.
Arguments:
- frame_rows: bfloat16 [2112, 28, 1024], P('owner', None, 'ingest'), may hold values from -32 to 32
- route_owner: int32 [2112], P('owner'), may hold values from 0 to 63, as said below
- route_slot: int32 [2112], P('owner'), may hold values from 0 to 32, as said below
- frames: int32 [2112], P('owner'), may hold values from 1 to 28, as said below
- kv_cache: bfloat16 [2112, 8, 70, 256], P('owner', 'ingest'), may hold values from -250 to 250
- conv_cache: bfloat16 [2112, 8, 1024], P('owner', None, 'ingest'), may hold values from -5 to 5
- mig_owner: int32 [2048], P('owner'), may hold values from 0 to 63, as said below
- ln1_gain: float32 [1024], replicated, may hold values from 0.1 to 1.9
- w_qkv: bfloat16 [1024, 8, 384], P(None, 'ingest'), may hold values from -0.1875 to 0.1875
- w_out: bfloat16 [1024, 1024], P('ingest'), may hold values from -0.1875 to 0.1875
- ln2_gain: float32 [1024], replicated, may hold values from 0.1 to 1.9
- w_pw1: bfloat16 [1024, 2, 1024], P(None, None, 'ingest'), may hold values from -0.1875 to 0.1875
- dw_weight: bfloat16 [9, 1024], P(None, 'ingest'), may hold values from -2 to 2
- bn_scale: float32 [1024], P('ingest'), may hold values from 0.1 to 1.9
- bn_shift: float32 [1024], P('ingest'), may hold values from -2.5 to 2.5
- w_pw2: bfloat16 [1024, 1024], P('ingest'), may hold values from -0.1875 to 0.1875
Outputs:
- layer_out: bfloat16 [2112, 28, 1024], P('owner', None, 'ingest')
- kv_next: bfloat16 [2112, 8, 70, 256], P('owner', 'ingest')
- conv_next: bfloat16 [2112, 8, 1024], P('owner', None, 'ingest')
Inputs may be any that keep to these rules, and one draw needn't show every extreme that they name: `route_owner`: every owner receives exactly 33 utterances. The utterances that one source device along owner (a block of 33 rows in arrival order) sends to one owner number at most 1, and some source device reaches that number. `route_slot`: the utterances sent to one owner have distinct slots. Every owner holds an utterance with 28 new frames. The utterance in old slot 1 + j of an owner moves to slot 1 + j of owner mig_owner; the 32 utterances of one owner go to 32 different other owners, and every owner receives exactly one utterance for each j.
All inputs are finite; a program needn't handle non-finite values.
Results may differ from a plain program's by a relative error of at most 0.01.
Values may be sent and summed in bfloat16 or wider, within the bound.
No kernel may reach another device: no remote copies, remote signals or barrier semaphores. Data moves between devices by JAX's collectives and lax.ppermute only.
A program may use at most 64 MiB of HBM per device.

v0:
```python
import jax
import jax.numpy as jnp
from jax import lax
from jax.sharding import PartitionSpec as P

BLOCKS = 2
norm_eps = 1e-05


def normalize(values, gain_cols):
    model_width = values.shape[-1]
    row_mean = jnp.sum(values, axis=-1, keepdims=True) / model_width
    spread = jnp.sum(values * values, axis=-1, keepdims=True) / model_width - row_mean * row_mean
    return ((values - row_mean) * lax.rsqrt(spread + norm_eps) * gain_cols).astype(jnp.bfloat16)


def one_hot_rows(table, rows):
    return jnp.dot(table.astype(jnp.bfloat16), rows, preferred_element_type=jnp.float32).astype(
        jnp.bfloat16
    )


def grouped_terms(left_groups, right_groups):
    terms = jnp.einsum(
        "grc,gcn->grn", left_groups, right_groups, preferred_element_type=jnp.float32
    ).astype(jnp.bfloat16)
    return jnp.sum(terms.astype(jnp.float32), axis=0)


def shards(
    frame_rows,
    route_owner,
    route_slot,
    frames,
    kv_cache,
    conv_cache,
    mig_owner,
    ln1_gain,
    w_qkv,
    w_out,
    ln2_gain,
    w_pw1,
    dw_weight,
    bn_scale,
    bn_shift,
    w_pw2,
):
    owners = lax.axis_size("owner")
    groups = lax.axis_size("ingest")
    me = lax.axis_index("ingest")
    utterances, frame_span, local_width = frame_rows.shape
    model_width = w_qkv.shape[0]
    head_dim = w_qkv.shape[2] // 3
    cache_len = kv_cache.shape[2]
    conv_len = conv_cache.shape[1]
    taps = dw_weight.shape[0]
    horizon = frame_span // BLOCKS
    moving = mig_owner.shape[0]
    settled = utterances - moving
    lanes = 128
    w_out_full = lax.all_gather(w_out, "ingest", axis=0, tiled=True)
    w_pw2_cols = lax.all_to_all(
        w_pw2.reshape(local_width, groups, local_width).transpose(1, 0, 2),
        "ingest",
        split_axis=0,
        concat_axis=0,
        tiled=True,
    )
    dest = jnp.arange(owners, dtype=jnp.int32)
    frame_flat = frame_rows.reshape(utterances, frame_span * local_width)
    slot_tag = jnp.broadcast_to((route_slot + 1).astype(jnp.bfloat16)[:, None], (utterances, lanes))
    frame_send = one_hot_rows(
        dest[:, None] == route_owner[None, :], jnp.concatenate([frame_flat, slot_tag], axis=1)
    )
    kv_width = cache_len * 2 * head_dim
    conv_width = conv_len * local_width
    mover_tag = jnp.broadcast_to(
        (jnp.arange(moving, dtype=jnp.int32) + 1).astype(jnp.bfloat16)[:, None], (moving, lanes)
    )
    cache_rows = jnp.concatenate(
        [
            kv_cache[settled:].reshape(moving, kv_width),
            conv_cache[settled:].reshape(moving, conv_width),
            mover_tag,
        ],
        axis=1,
    )
    cache_send = one_hot_rows(dest[:, None] == mig_owner[None, :], cache_rows)
    frame_cols = frame_send.shape[1]
    arrived = lax.all_to_all(
        jnp.concatenate([frame_send, cache_send], axis=1),
        "owner",
        split_axis=0,
        concat_axis=0,
        tiled=True,
    )
    frame_part = frame_span * local_width
    got_slot = arrived[:, frame_part].astype(jnp.int32)
    slots = jnp.arange(utterances, dtype=jnp.int32)
    arranged = one_hot_rows(
        slots[:, None] + 1 == got_slot[None, :], arrived[:, :frame_part]
    ).reshape(utterances, frame_span, local_width)
    got_mover = arrived[:, frame_cols + kv_width + conv_width].astype(jnp.int32)
    movers = jnp.arange(moving, dtype=jnp.int32)
    moved = one_hot_rows(
        movers[:, None] + 1 == got_mover[None, :],
        arrived[:, frame_cols : frame_cols + kv_width + conv_width],
    )
    kv_state = jnp.concatenate(
        [
            kv_cache[:settled].reshape(settled, cache_len, 2 * head_dim),
            moved[:, :kv_width].reshape(moving, cache_len, 2 * head_dim),
        ],
        axis=0,
    )
    conv_state = jnp.concatenate(
        [conv_cache[:settled], moved[:, kv_width:].reshape(moving, conv_len, local_width)], axis=0
    )
    x_all = lax.all_gather(arranged, "ingest", axis=0, tiled=False)
    x_rows = x_all.transpose(1, 2, 0, 3).reshape(utterances, frame_span, model_width)
    x_rows = x_rows.astype(jnp.float32)
    normed = normalize(x_rows, ln1_gain)
    projected = jnp.dot(
        normed, w_qkv.reshape(model_width, 3 * head_dim), preferred_element_type=jnp.float32
    )
    queries = projected[..., :head_dim].astype(jnp.bfloat16)
    fresh = projected[..., head_dim:].astype(jnp.bfloat16)
    memory = jnp.concatenate([kv_state, fresh], axis=1)
    keys_total = memory.shape[1]
    scores = jnp.einsum(
        "sqd,skd->sqk", queries, memory[..., :head_dim], preferred_element_type=jnp.float32
    ) * head_dim ** (-0.5)
    frame_index = jnp.arange(frame_span, dtype=jnp.int32)
    block_of = frame_index // horizon
    low = block_of * horizon
    high = cache_len + jnp.minimum(frames[:, None], (block_of[None, :] + 1) * horizon)
    position = jnp.arange(keys_total, dtype=jnp.int32)
    live_keys = (position[None, None, :] >= low[None, :, None]) & (
        position[None, None, :] < high[:, :, None]
    )
    scores = jnp.where(live_keys, scores, -1e30)
    row_max = jnp.max(scores, axis=-1, keepdims=True)
    weights = jnp.exp(scores - row_max)
    probabilities = (weights / jnp.sum(weights, axis=-1, keepdims=True)).astype(jnp.bfloat16)
    context = jnp.einsum(
        "sqk,skd->sqd", probabilities, memory[..., head_dim:], preferred_element_type=jnp.float32
    ).astype(jnp.bfloat16)
    ctx_all = lax.all_gather(context, "ingest", axis=0, tiled=False)
    row_count = utterances * frame_span
    attn = grouped_terms(
        ctx_all.reshape(groups, row_count, head_dim),
        w_out_full.reshape(groups, head_dim, model_width),
    )
    residual = x_rows.reshape(row_count, model_width) + attn
    normed2 = normalize(residual, ln2_gain)
    mixed = jnp.dot(
        normed2, w_pw1.reshape(model_width, 2 * local_width), preferred_element_type=jnp.float32
    )
    glu_out = (mixed[:, :local_width] * jax.nn.sigmoid(mixed[:, local_width:])).astype(jnp.bfloat16)
    glu_out = glu_out.reshape(utterances, frame_span, local_width)
    joined = jnp.concatenate([conv_state, glu_out], axis=1)
    joined_f = joined.astype(jnp.float32)
    running = jnp.zeros((utterances, frame_span, local_width), jnp.float32)
    for tap_index in range(taps):
        running = running + joined_f[:, tap_index : tap_index + frame_span, :] * dw_weight[
            tap_index
        ].astype(jnp.float32)
    activated = jax.nn.silu(running * bn_scale + bn_shift).astype(jnp.bfloat16)
    act_all = lax.all_gather(activated, "ingest", axis=0, tiled=False)
    conv_terms = grouped_terms(act_all.reshape(groups, row_count, local_width), w_pw2_cols)
    residual_own = lax.dynamic_slice_in_dim(residual, me * local_width, local_width, 1)
    result = (residual_own + conv_terms).reshape(utterances, frame_span, local_width)
    live_rows = frame_index[None, :] < frames[:, None]
    layer_out = jnp.where(live_rows[:, :, None], result, 0.0).astype(jnp.bfloat16)
    keep = jnp.arange(cache_len, dtype=jnp.int32)
    kv_pick = position[None, None, :] == keep[None, :, None] + frames[:, None, None]
    kv_next = jnp.einsum(
        "srp,spd->srd", kv_pick.astype(jnp.bfloat16), memory, preferred_element_type=jnp.float32
    ).astype(jnp.bfloat16)
    conv_keep = jnp.arange(conv_len, dtype=jnp.int32)
    conv_pos = jnp.arange(joined.shape[1], dtype=jnp.int32)
    conv_pick = conv_pos[None, None, :] == conv_keep[None, :, None] + frames[:, None, None]
    conv_next = jnp.einsum(
        "srp,spd->srd", conv_pick.astype(jnp.bfloat16), joined, preferred_element_type=jnp.float32
    ).astype(jnp.bfloat16)
    return (layer_out, kv_next.reshape(kv_cache.shape), conv_next)


def solution(mesh):
    in_specs = (
        P("owner", None, "ingest"),
        P("owner"),
        P("owner"),
        P("owner"),
        P("owner", "ingest", None, None),
        P("owner", None, "ingest"),
        P("owner"),
        P(),
        P(None, "ingest", None),
        P("ingest", None),
        P(),
        P(None, None, "ingest"),
        P(None, "ingest"),
        P("ingest"),
        P("ingest"),
        P("ingest", None),
    )
    out_specs = (
        P("owner", None, "ingest"),
        P("owner", "ingest", None, None),
        P("owner", None, "ingest"),
    )
    return jax.shard_map(shards, mesh=mesh, in_specs=in_specs, out_specs=out_specs, check_vma=False)
```

profile of v0, /device:TPU:1, one launch (start us, length us, event | category | flops | bytes accessed | tf_op | source)
XLA Modules:
  0.0 387.9 jit_solution(17638379592714041639)
XLA Ops:
  12.8 5.4 %reduce.8 = bf16[64,22784]{1,0:T(8,128)(2,1)} reduce(bf16[64,1,22784]{2,0,1:T(8,128)(2,1)} %maximum_bitcast_fusion, bf16[]{:T(256)} %broadcast.254), dimensions={1}, to_apply=%copy.30.reduce_sub_computation | reduce | bytes 5832706 | tf_op jit(solution)/shard_map/all_to_all | solution.py:90
  18.2 4.4 %reshape.407 = bf16[64,2,11392]{2,1,0:T(2,128)(2,1)} reshape(bf16[64,22784]{1,0:T(8,128)(2,1)} %reduce.8) | data formatting | bytes 5832704
  22.6 19.3 %all-to-all-start = ((bf16[64,2,11392]{2,1,0:T(2,128)(2,1)}), bf16[64,2,11392]{2,1,0:T(2,128)(2,1)}, u32[]{:S(2)}, u32[]{:S(2)}) async-start(bf16[64,2,11392]{2,1,0:T(2,128)(2,1)} %reshape.407), calls=%async_computation | async-start | bytes 5832704 | tf_op jit(solution)/shard_map/all_to_all | solution.py:90
  42.0 127.4 %all-to-all-done = bf16[64,2,11392]{2,1,0:T(2,128)(2,1)} async-done(((bf16[64,2,11392]{2,1,0:T(2,128)(2,1)}), bf16[64,2,11392]{2,1,0:T(2,128)(2,1)}, u32[]{:S(2)}, u32[]{:S(2)}) %all-to-all-start) | async-done | bytes 2916384 | tf_op jit(solution)/shard_map/all_to_all | solution.py:90
  169.5 16.8 %reshape.408 = bf16[64,1,22784]{2,1,0:T(2,128)(2,1)} reshape(bf16[64,2,11392]{2,1,0:T(2,128)(2,1)} %all-to-all-done) | data formatting | bytes 5832704
  186.2 3.1 copy.57
  192.5 2.2 convolution_convert_fusion.1
  195.9 2.5 reshape.378
  198.4 26.5 %all-gather.7.cloned.1.call-done = bf16[8,33,28,128]{3,2,1,0:T(8,128)(2,1)} async-done(((bf16[1,33,28,128]{3,2,1,0:T(8,128)(2,1)}), bf16[8,33,28,128]{3,2,1,0:T(8,128)(2,1)}) %all-gather.7.cloned.1.call-update) | async-done | bytes 1892368 | tf_op jit(solution)/shard_map/all_gather | solution.py:119
  224.9 5.3 %bitcast_reduce_fusion = (f32[33,28]{1,0:T(8,128)S(1)}, f32[33,28]{1,0:T(8,128)S(1)}) fusion(bf16[8,33,28,128]{3,2,1,0:T(8,128)(2,1)} %all-gather.7.cloned.1.call-done), kind=kLoop, calls=%fused_computation.9 | loop fusion | flops 3782856 | bytes 1899744 | tf_op jit(solution)/shard_map/reduce_sum | solution.py:12
  230.3 5.5 %fusion.3 = bf16[33,28,8,128]{3,2,1,0:T(8,128)(2,1)} fusion(f32[8,128]{1,0:T(8,128)S(1)} %bitcast.128, f32[33,28]{1,0:T(8,128)S(1)} %get-tuple-element.24, f32[33,28]{1,0:T(8,128)S(1)} %get-tuple-element.23, bf16[8,33,28,128]{3,2,1,0:T(8,128)(2,1)S(1)} %copy-done.2), kind=kLoop, calls=%fused_computation.13 | loop fusion | flops 4730880 | bytes 3796192 | tf_op jit(solution)/shard_map/convert_element_type | solution.py:14
  235.7 4.1 %convert_element_type.219 = bf16[33,28,1024]{2,1,0:T(8,128)(2,1)} reshape(bf16[33,28,8,128]{3,2,1,0:T(8,128)(2,1)} %fusion.3) | data formatting | bytes 3784704 | tf_op jit(solution)/shard_map/convert_element_type | solution.py:14
  239.9 3.0 convolution_convert_fusion.5
  245.5 3.8 convolution_convert_fusion.6
  251.8 31.2 %all-gather.11.cloned.1.call-done = bf16[264,28,128]{2,1,0:T(8,128)(2,1)} async-done(((bf16[33,28,128]{2,1,0:T(8,128)(2,1)}), bf16[264,28,128]{2,1,0:T(8,128)(2,1)}) %all-gather.11.cloned.1.call-update) | async-done | bytes 1892368 | tf_op jit(solution)/shard_map/all_gather | solution.py:148
  283.0 3.6 reshape.379
  286.6 32.0 %all-gather.9.cloned.1.call-done = bf16[1024,1024]{1,0:T(8,128)(2,1)} async-done(((bf16[128,1024]{1,0:T(8,128)(2,1)}), bf16[1024,1024]{1,0:T(8,128)(2,1)}) %all-gather.9.cloned.1.call-update) | async-done | bytes 2097168 | tf_op jit(solution)/shard_map/all_gather | solution.py:61
  318.6 6.6 %convert_reduce_fusion = f32[924,1024]{1,0:T(8,128)S(1)} fusion(bf16[8,924,128]{2,1,0:T(8,128)(2,1)} %reshape.379, bf16[8,128,1024]{2,1,0:T(8,128)(2,1)} %bitcast.129), kind=kOutput, calls=%fused_computation.1 | convolution fusion | flops 1959530496 | bytes 7774208 | tf_op jit(solution)/shard_map/grc,gcn->grn/dot_general | solution.py:24
  327.5 3.6 fusion.6
  331.1 5.0 %multiply_convert_fusion = bf16[33,28,8,128]{3,2,1,0:T(8,128)(2,1)S(1)} fusion(f32[8,128]{1,0:T(8,128)S(1)} %bitcast.127, f32[33,28]{1,0:T(8,128)S(1)} %get-tuple-element.22, f32[33,28]{1,0:T(8,128)S(1)} %get-tuple-element.21, f32[33,28,8,128]{3,2,1,0:T(8,128)S(1)} %bitcast.106, bf16[8,33,28,128]{3,2,1,0:T(8,128)(2,1)S(1)} %copy-done.2), kind=kLoop, calls=%fused_computation.15 | loop fusion | flops 5677056 | bytes 7580896 | tf_op jit(solution)/shard_map/convert_element_type | solution.py:14
  343.4 4.3 %all-to-all-start.1 = ((bf16[8,128,128]{2,1,0:T(8,128)(2,1)}), bf16[8,128,128]{2,1,0:T(8,128)(2,1)}, u32[]{:S(2)}, u32[]{:S(2)}) async-start(bf16[8,128,128]{2,1,0:T(8,128)(2,1)} %bitcast.18), calls=%async_computation.1 | async-start | bytes 524288 | tf_op jit(solution)/shard_map/all_to_all | solution.py:62
  351.4 2.8 copy.39
  355.0 19.9 %all-gather.13.cloned.1.call-done = bf16[264,28,128]{2,1,0:T(8,128)(2,1)} async-done(((bf16[33,28,128]{2,1,0:T(8,128)(2,1)}), bf16[264,28,128]{2,1,0:T(8,128)(2,1)}) %all-gather.13.cloned.1.call-update) | async-done | bytes 1892368 | tf_op jit(solution)/shard_map/all_gather | solution.py:169
  374.9 2.5 reshape.384
  (121 shorter events, 32.6 us)
Async XLA Ops:
  7.2 232.7 %copy-start = (bf16[1024,1,384]{2,0,1:T(8,128)(2,1)S(1)}, bf16[1024,1,384]{2,0,1:T(8,128)(2,1)}, u32[]{:S(2)}) copy-start(bf16[1024,1,384]{2,0,1:T(8,128)(2,1)} %param.24) | copy-start | bytes 2359300
  7.2 2.0 copy-start.26
  7.2 2.1 copy-start.23
  7.3 2.5 copy-start.24
  22.6 146.9 %all-to-all-start = ((bf16[64,2,11392]{2,1,0:T(2,128)(2,1)}), bf16[64,2,11392]{2,1,0:T(2,128)(2,1)}, u32[]{:S(2)}, u32[]{:S(2)}) async-start(bf16[64,2,11392]{2,1,0:T(2,128)(2,1)} %reshape.407), calls=%async_computation | async-start | bytes 5832704 | tf_op jit(solution)/shard_map/all_to_all | solution.py:90
  42.0 182.9 %all-gather.7.cloned.1.call-start = ((), (), s32[]{:S(2)}) async-start(), calls=%async_computation.2 | async-start | bytes 2433024 | tf_op jit(solution)/shard_map/all_gather | solution.py:119
  186.2 6.2 %copy-start.13 = (s32[33]{0:T(128)S(1)}, s32[33]{0:T(128)}, u32[]{:S(2)}) copy-start(s32[33]{0:T(128)} %param.19) | copy-start | bytes 400
  186.2 6.2 %copy-start.8 = (bf16[33,1,70,256]{3,2,1,0:T(8,128)(2,1)S(1)}, bf16[33,1,70,256]{3,2,1,0:T(8,128)(2,1)}, u32[]{:S(2)}) copy-start(bf16[33,1,70,256]{3,2,1,0:T(8,128)(2,1)} %param.20) | copy-start | bytes 3548164
  192.1 90.9 %all-gather.11.cloned.1.call-start = ((), (), s32[]{:S(2)}) async-start(), calls=%async_computation.4 | async-start | bytes 2433024 | tf_op jit(solution)/shard_map/all_gather | solution.py:148
  194.7 3.7 copy-start.4
  195.9 34.4 %copy-start.16 = (f32[1024]{0:T(1024)S(1)}, f32[1024]{0:T(1024)}, u32[]{:S(2)}) copy-start(f32[1024]{0:T(1024)} %param.23) | copy-start | bytes 12292
  224.9 5.4 %copy-start.2 = (bf16[8,33,28,128]{3,2,1,0:T(8,128)(2,1)S(1)}, bf16[8,33,28,128]{3,2,1,0:T(8,128)(2,1)}, u32[]{:S(2)}) copy-start(bf16[8,33,28,128]{3,2,1,0:T(8,128)(2,1)} %all-gather.7.cloned.1.call-done) | copy-start | bytes 5677060
  239.9 3.1 copy-start.6
  245.1 5.2 %copy-start.12 = (bf16[33,8,128]{2,1,0:T(8,128)(2,1)S(1)}, bf16[33,8,128]{2,1,0:T(8,128)(2,1)}, u32[]{:S(2)}) copy-start(bf16[33,8,128]{2,1,0:T(8,128)(2,1)} %param.21) | copy-start | bytes 202756
  245.1 5.2 %copy-start.14 = (bf16[9,128]{1,0:T(8,128)(2,1)S(1)}, bf16[9,128]{1,0:T(8,128)(2,1)}, u32[]{:S(2)}) copy-start(bf16[9,128]{1,0:T(8,128)(2,1)} %param.28) | copy-start | bytes 6916
  249.3 69.4 %all-gather.9.cloned.1.call-start = ((), (), s32[]{:S(2)}) async-start(), calls=%async_computation.3 | async-start | bytes 2359296 | tf_op jit(solution)/shard_map/all_gather | solution.py:61
  250.0 124.9 %all-gather.13.cloned.1.call-start = ((), (), s32[]{:S(2)}) async-start(), calls=%async_computation.5 | async-start | bytes 2433024 | tf_op jit(solution)/shard_map/all_gather | solution.py:169
  327.4 3.6 copy-start.15
  338.0 2.0 copy-start.17
  338.0 2.0 copy-start.18
  338.0 2.0 copy-start.19
  343.4 34.0 %all-to-all-start.1 = ((bf16[8,128,128]{2,1,0:T(8,128)(2,1)}), bf16[8,128,128]{2,1,0:T(8,128)(2,1)}, u32[]{:S(2)}, u32[]{:S(2)}) async-start(bf16[8,128,128]{2,1,0:T(8,128)(2,1)} %bitcast.18), calls=%async_computation.1 | async-start | bytes 524288 | tf_op jit(solution)/shard_map/all_to_all | solution.py:62
  351.3 2.8 copy-start.10
  374.9 6.4 %copy-start.1 = (bf16[1024,1,384]{2,0,1:T(8,128)(2,1)S(1)}, bf16[1024,1,384]{2,0,1:T(8,128)(2,1)}, u32[]{:S(2)}) copy-start(bf16[1024,1,384]{2,0,1:T(8,128)(2,1)} %param.24) | copy-start | bytes 2359300
  (11 other events, 18.3 us)
Sparse Core Ops, SparseCore 0:
  192.2 32.6 all-gather.6
  249.4 33.5 all-gather.10
  285.2 33.4 all-gather.8
  341.5 33.3 all-gather.12
where the time goes:
time: 389 us; the launch traced here: 388 us
  waiting for transfers between devices  238 us (61%)
  local copies, waits for them, and re-layouts  54.9 us (14%)
  other arithmetic  34 us (9%)
  starting transfers between devices  24.2 us (6%)
  matrix products  22.6 us (6%)
  between operations  14.4 us (4%)
    all_to_all x1, waiting for transfers between devices, shards(): lax.all_to_all(jnp.concatenate([frame_send, cache_send], axis=1), 'owner'...  127 us
    unnamed x70, local copies, waits for them, and re-layouts  36.2 us
    all_gather x1, waiting for transfers between devices, shards(): w_out_full = lax.all_gather(w_out, 'ingest', axis=0, tiled=True)  32 us
    all_gather x1, waiting for transfers between devices, shards(): ctx_all = lax.all_gather(context, 'ingest', axis=0, tiled=False)  31.2 us
    all_gather x1, waiting for transfers between devices, shards(): x_all = lax.all_gather(arranged, 'ingest', axis=0, tiled=False)  26.5 us
    all_gather x1, waiting for transfers between devices, shards(): act_all = lax.all_gather(activated, 'ingest', axis=0, tiled=False)  19.9 us
    all_to_all x1, starting transfers between devices, shards(): lax.all_to_all(jnp.concatenate([frame_send, cache_send], axis=1), 'owner'...  19.3 us
    convert_element_type x2, other arithmetic, normalize(): ((values - row_mean) * lax.rsqrt(spread + norm_eps) * gain_cols).astype(j...  10.5 us
  transfers between devices with their start and end apart: 6, of which 5 were waited for; matrix products, arithmetic and copies ran while one was open for 6% of the time, Pallas kernels for 0%

commit v1 on v0

--- a/solution.py
+++ b/solution.py
@@ -5,6 +5,34 @@
 
 BLOCKS = 2
 norm_eps = 1e-05
+
+
+def _cover_cells(inner_x):
+    prior, outer, current_block = (
+        lax.axis_size("ingest"),
+        lax.axis_index("ingest"),
+        inner_x.shape[0],
+    )
+    heap = tuple((q * prior if hop_no == 0 else q for hop_no, q in enumerate(inner_x.shape)))
+    y2 = built = inner_x
+    state_next = lax.dynamic_update_slice_in_dim(
+        jnp.zeros(heap, inner_x.dtype), inner_x, outer * current_block, axis=0
+    )
+    for jj in [*range(1, prior // 2 + 1)]:
+        y2 = lax.ppermute(
+            y2, "ingest", tuple(((hop_no, (hop_no + 1) % prior) for hop_no in range(prior)))
+        )
+        state_next = lax.dynamic_update_slice_in_dim(
+            state_next, y2, (outer - jj) % prior * current_block, axis=0
+        )
+        if 2 * jj < prior:
+            built = lax.ppermute(
+                built, "ingest", tuple(((hop_no, (hop_no - 1) % prior) for hop_no in range(prior)))
+            )
+            state_next = lax.dynamic_update_slice_in_dim(
+                state_next, built, (outer + jj) % prior * current_block, axis=0
+            )
+    return state_next
 
 
 def normalize(values, gain_cols):
@@ -58,7 +86,7 @@
     moving = mig_owner.shape[0]
     settled = utterances - moving
     lanes = 128
-    w_out_full = lax.all_gather(w_out, "ingest", axis=0, tiled=True)
+    w_out_full = _cover_cells(w_out)
     w_pw2_cols = lax.all_to_all(
         w_pw2.reshape(local_width, groups, local_width).transpose(1, 0, 2),
         "ingest",

time: 389 us -> 359 us (0.923)
  waiting for transfers between devices: 238 us -> 189 us
  local copies, waits for them, and re-layouts: 54.9 us -> 64.9 us
  starting transfers between devices: 24.2 us -> 32 us
    all_gather x1 -> x0, waiting for transfers between devices: 32 us -> none  [shards(): w_out_full = lax.all_gather(w_out, 'ingest', axis=0, tiled=True)]
    all_gather x1, waiting for transfers between devices: 31.2 us -> 8.61 us  [shards(): ctx_all = lax.all_gather(context, 'ingest', axis=0, tiled=False)]
    ppermute x0 -> x7, starting transfers between devices: none -> 8.1 us  [the longest x4 4.25 us: _cover_cells(): lax.ppermute(y2, 'ingest', tuple(((hop_no, (hop_no + 1) % prior) for hop_...]
    dynamic_update_slice x0 -> x8, local copies, waits for them, and re-layouts: none -> 7.71 us  [the longest x4 3.82 us: _cover_cells(): lax.dynamic_update_slice_in_dim(state_next, y2, (outer - jj) % prior * cu...]
    ppermute x0 -> x7, waiting for transfers between devices: none -> 7.27 us  [the longest x4 7.26 us: _cover_cells(): lax.ppermute(y2, 'ingest', tuple(((hop_no, (hop_no + 1) % prior) for hop_...]
    unnamed x70 -> x72, local copies, waits for them, and re-layouts: 36.2 us -> 36.1 us
  transfers between devices with their start and end apart: 6 -> 12, of which waited for: 5 -> 6; matrix products, arithmetic and copies ran while one was open for 6% -> 8% of each run, Pallas kernels for 0% -> 0%
where the time goes in v1:
time: 359 us; the launch traced here: 357 us
  waiting for transfers between devices  189 us (53%)
  local copies, waits for them, and re-layouts  64.9 us (18%)
  other arithmetic  34 us (9%)
  starting transfers between devices  32 us (9%)
  matrix products  22.6 us (6%)
  between operations  14.3 us (4%)
    all_to_all x1, waiting for transfers between devices, shards(): lax.all_to_all(jnp.concatenate([frame_send, cache_send], axis=1), 'owner'...  127 us
    unnamed x72, local copies, waits for them, and re-layouts  36.1 us
    all_gather x1, waiting for transfers between devices, shards(): x_all = lax.all_gather(arranged, 'ingest', axis=0, tiled=False)  26.5 us
    all_gather x1, waiting for transfers between devices, shards(): act_all = lax.all_gather(activated, 'ingest', axis=0, tiled=False)  19.5 us
    all_to_all x1, starting transfers between devices, shards(): lax.all_to_all(jnp.concatenate([frame_send, cache_send], axis=1), 'owner'...  19.3 us
    convert_element_type x2, other arithmetic, normalize(): ((values - row_mean) * lax.rsqrt(spread + norm_eps) * gain_cols).astype(j...  10.5 us
    reduce_sum x2, other arithmetic, normalize(): row_mean = jnp.sum(values, axis=-1, keepdims=True) / model_width  8.92 us
    all_gather x1, waiting for transfers between devices, shards(): ctx_all = lax.all_gather(context, 'ingest', axis=0, tiled=False)  8.61 us
  transfers between devices with their start and end apart: 12, of which 6 were waited for; matrix products, arithmetic and copies ran while one was open for 8% of the time, Pallas kernels for 0%

profile of v1, /device:TPU:1, one launch (start us, length us, event | category | flops | bytes accessed | tf_op | source)
XLA Modules:
  0.0 357.2 jit_solution(10079481334621019486)
XLA Ops:
  12.8 5.4 %reduce.8 = bf16[64,22784]{1,0:T(8,128)(2,1)} reduce(bf16[64,1,22784]{2,0,1:T(8,128)(2,1)} %maximum_bitcast_fusion, bf16[]{:T(256)} %broadcast.261), dimensions={1}, to_apply=%copy.30.reduce_sub_computation | reduce | bytes 5832706 | tf_op jit(solution)/shard_map/all_to_all | solution.py:118
  18.2 4.4 %reshape.407 = bf16[64,2,11392]{2,1,0:T(2,128)(2,1)} reshape(bf16[64,22784]{1,0:T(8,128)(2,1)} %reduce.8) | data formatting | bytes 5832704
  22.6 19.3 %all-to-all-start = ((bf16[64,2,11392]{2,1,0:T(2,128)(2,1)}), bf16[64,2,11392]{2,1,0:T(2,128)(2,1)}, u32[]{:S(2)}, u32[]{:S(2)}) async-start(bf16[64,2,11392]{2,1,0:T(2,128)(2,1)} %reshape.407), calls=%async_computation | async-start | bytes 5832704 | tf_op jit(solution)/shard_map/all_to_all | solution.py:118
  42.0 127.4 %all-to-all-done = bf16[64,2,11392]{2,1,0:T(2,128)(2,1)} async-done(((bf16[64,2,11392]{2,1,0:T(2,128)(2,1)}), bf16[64,2,11392]{2,1,0:T(2,128)(2,1)}, u32[]{:S(2)}, u32[]{:S(2)}) %all-to-all-start) | async-done | bytes 2916384 | tf_op jit(solution)/shard_map/all_to_all | solution.py:118
  169.5 16.8 %reshape.408 = bf16[64,1,22784]{2,1,0:T(2,128)(2,1)} reshape(bf16[64,2,11392]{2,1,0:T(2,128)(2,1)} %all-to-all-done) | data formatting | bytes 5832704
  186.2 3.1 copy.57
  195.9 2.5 reshape.378
  198.4 26.5 %all-gather.6.cloned.1.call-done = bf16[8,33,28,128]{3,2,1,0:T(8,128)(2,1)} async-done(((bf16[1,33,28,128]{3,2,1,0:T(8,128)(2,1)}), bf16[8,33,28,128]{3,2,1,0:T(8,128)(2,1)}) %all-gather.6.cloned.1.call-update) | async-done | bytes 1892368 | tf_op jit(solution)/shard_map/all_gather | solution.py:147
  224.9 5.3 %bitcast_reduce_fusion = (f32[33,28]{1,0:T(8,128)S(1)}, f32[33,28]{1,0:T(8,128)S(1)}) fusion(bf16[8,33,28,128]{3,2,1,0:T(8,128)(2,1)} %all-gather.6.cloned.1.call-done), kind=kLoop, calls=%fused_computation.9 | loop fusion | flops 3782856 | bytes 1899744 | tf_op jit(solution)/shard_map/reduce_sum | solution.py:40
  230.2 5.5 %fusion.3 = bf16[33,28,8,128]{3,2,1,0:T(8,128)(2,1)} fusion(f32[8,128]{1,0:T(8,128)S(1)} %bitcast.128, f32[33,28]{1,0:T(8,128)S(1)} %get-tuple-element.24, f32[33,28]{1,0:T(8,128)S(1)} %get-tuple-element.23, bf16[8,33,28,128]{3,2,1,0:T(8,128)(2,1)S(1)} %copy-done.2), kind=kLoop, calls=%fused_computation.13 | loop fusion | flops 4730880 | bytes 3796192 | tf_op jit(solution)/shard_map/convert_element_type | solution.py:42
  235.7 4.1 %convert_element_type.219 = bf16[33,28,1024]{2,1,0:T(8,128)(2,1)} reshape(bf16[33,28,8,128]{3,2,1,0:T(8,128)(2,1)} %fusion.3) | data formatting | bytes 3784704 | tf_op jit(solution)/shard_map/convert_element_type | solution.py:42
  239.8 3.0 convolution_convert_fusion.5
  245.4 3.8 %convolution_convert_fusion.6 = bf16[33,28,128]{2,1,0:T(8,128)(2,1)} fusion(bf16[33,98,256]{2,1,0:T(8,128)(2,1)} %copy-done.9, f32[33,28]{1,0:T(8,128)S(1)} %fusion.61, f32[33,28,98]{2,1,0:T(8,128)S(1)} %fusion.10), kind=kOutput, calls=%fused_computation.35 | convolution fusion | flops 23572260 | bytes 2216960 | tf_op jit(solution)/shard_map/sqk,skd->sqd/dot_general | solution.py:173
  249.8 3.4 collective-permute-done
  270.6 3.9 %collective-permute-done.6 = bf16[128,1024]{1,0:T(8,128)(2,1)S(1)} collective-permute-done((bf16[128,1024]{1,0:T(8,128)(2,1)S(1)}, bf16[128,1024]{1,0:T(8,128)(2,1)S(1)}, u32[]{:S(2)}, u32[]{:S(2)}) %collective-permute-start.6) | collective-permute-done | bytes 262176 | tf_op jit(solution)/shard_map/ppermute | solution.py:22
  276.1 8.6 %all-gather.8.cloned.1.call-done = bf16[264,28,128]{2,1,0:T(8,128)(2,1)} async-done(((bf16[33,28,128]{2,1,0:T(8,128)(2,1)}), bf16[264,28,128]{2,1,0:T(8,128)(2,1)}) %all-gather.8.cloned.1.call-update) | async-done | bytes 1892368 | tf_op jit(solution)/shard_map/all_gather | solution.py:176
  284.7 3.7 %reshape.379 = bf16[8,924,128]{2,1,0:T(8,128)(2,1)} reshape(bf16[264,28,128]{2,1,0:T(8,128)(2,1)} %all-gather.8.cloned.1.call-done) | data formatting | bytes 3784704 | tf_op jit(solution)/shard_map/reshape | solution.py:179
  288.3 6.6 %convert_reduce_fusion = f32[924,1024]{1,0:T(8,128)S(1)} fusion(bf16[8,924,128]{2,1,0:T(8,128)(2,1)} %reshape.379, bf16[8,128,1024]{2,1,0:T(8,128)(2,1)} %bitcast.6), kind=kOutput, calls=%fused_computation.1 | convolution fusion | flops 1959530496 | bytes 7774208 | tf_op jit(solution)/shard_map/grc,gcn->grn/dot_general | solution.py:52
  297.1 3.6 %fusion.6 = (f32[33,28]{1,0:T(8,128)S(1)}, f32[33,28]{1,0:T(8,128)S(1)}) fusion(f32[33,28,8,128]{3,2,1,0:T(8,128)S(1)} %bitcast.105, bf16[8,33,28,128]{3,2,1,0:T(8,128)(2,1)S(1)} %copy-done.2), kind=kLoop, calls=%fused_computation.22 | loop fusion | flops 4729032 | bytes 5684448 | tf_op jit(solution)/shard_map/reduce_sum | solution.py:40
  300.8 5.0 %multiply_convert_fusion = bf16[33,28,8,128]{3,2,1,0:T(8,128)(2,1)S(1)} fusion(f32[8,128]{1,0:T(8,128)S(1)} %bitcast.127, f32[33,28]{1,0:T(8,128)S(1)} %get-tuple-element.22, f32[33,28]{1,0:T(8,128)S(1)} %get-tuple-element.21, f32[33,28,8,128]{3,2,1,0:T(8,128)S(1)} %bitcast.106, bf16[8,33,28,128]{3,2,1,0:T(8,128)(2,1)S(1)} %copy-done.2), kind=kLoop, calls=%fused_computation.15 | loop fusion | flops 5677056 | bytes 7580896 | tf_op jit(solution)/shard_map/convert_element_type | solution.py:42
  313.1 4.3 %all-to-all-start.1 = ((bf16[8,128,128]{2,1,0:T(8,128)(2,1)}), bf16[8,128,128]{2,1,0:T(8,128)(2,1)}, u32[]{:S(2)}, u32[]{:S(2)}) async-start(bf16[8,128,128]{2,1,0:T(8,128)(2,1)} %bitcast.18), calls=%async_computation.1 | async-start | bytes 524288 | tf_op jit(solution)/shard_map/all_to_all | solution.py:90
  321.1 2.7 copy.39
  324.7 19.5 %all-gather.10.cloned.1.call-done = bf16[264,28,128]{2,1,0:T(8,128)(2,1)} async-done(((bf16[33,28,128]{2,1,0:T(8,128)(2,1)}), bf16[264,28,128]{2,1,0:T(8,128)(2,1)}) %all-gather.10.cloned.1.call-update) | async-done | bytes 1892368 | tf_op jit(solution)/shard_map/all_gather | solution.py:197
  344.2 2.5 reshape.384
  (143 shorter events, 52.0 us)
Async XLA Ops:
  7.2 232.7 %copy-start = (bf16[1024,1,384]{2,0,1:T(8,128)(2,1)S(1)}, bf16[1024,1,384]{2,0,1:T(8,128)(2,1)}, u32[]{:S(2)}) copy-start(bf16[1024,1,384]{2,0,1:T(8,128)(2,1)} %param.24) | copy-start | bytes 2359300
  22.6 146.9 %all-to-all-start = ((bf16[64,2,11392]{2,1,0:T(2,128)(2,1)}), bf16[64,2,11392]{2,1,0:T(2,128)(2,1)}, u32[]{:S(2)}, u32[]{:S(2)}) async-start(bf16[64,2,11392]{2,1,0:T(2,128)(2,1)} %reshape.407), calls=%async_computation | async-start | bytes 5832704 | tf_op jit(solution)/shard_map/all_to_all | solution.py:118
  41.9 182.9 %all-gather.6.cloned.1.call-start = ((), (), s32[]{:S(2)}) async-start(), calls=%async_computation.2 | async-start | bytes 2433024 | tf_op jit(solution)/shard_map/all_gather | solution.py:147
  186.2 6.2 %copy-start.13 = (s32[33]{0:T(128)S(1)}, s32[33]{0:T(128)}, u32[]{:S(2)}) copy-start(s32[33]{0:T(128)} %param.19) | copy-start | bytes 400
  186.2 6.2 %copy-start.8 = (bf16[33,1,70,256]{3,2,1,0:T(8,128)(2,1)S(1)}, bf16[33,1,70,256]{3,2,1,0:T(8,128)(2,1)}, u32[]{:S(2)}) copy-start(bf16[33,1,70,256]{3,2,1,0:T(8,128)(2,1)} %param.20) | copy-start | bytes 3548164
  192.0 92.6 %all-gather.8.cloned.1.call-start = ((), (), s32[]{:S(2)}) async-start(), calls=%async_computation.3 | async-start | bytes 2433024 | tf_op jit(solution)/shard_map/all_gather | solution.py:176
  194.7 3.7 %copy-start.4 = (bf16[32,18944]{1,0:T(8,128)(2,1)}, bf16[32,18944]{1,0:T(8,128)(2,1)S(1)}, u32[]{:S(2)}) copy-start(bf16[32,18944]{1,0:T(8,128)(2,1)S(1)} %convolution_convert_fusion.1) | copy-start | bytes 3637252
  195.9 34.4 %copy-start.16 = (f32[1024]{0:T(1024)S(1)}, f32[1024]{0:T(1024)}, u32[]{:S(2)}) copy-start(f32[1024]{0:T(1024)} %param.23) | copy-start | bytes 12292
  224.9 5.4 %copy-start.2 = (bf16[8,33,28,128]{3,2,1,0:T(8,128)(2,1)S(1)}, bf16[8,33,28,128]{3,2,1,0:T(8,128)(2,1)}, u32[]{:S(2)}) copy-start(bf16[8,33,28,128]{3,2,1,0:T(8,128)(2,1)} %all-gather.6.cloned.1.call-done) | copy-start | bytes 5677060
  239.8 3.1 copy-start.6
  245.0 10.5 %copy-start.14 = (bf16[9,128]{1,0:T(8,128)(2,1)S(1)}, bf16[9,128]{1,0:T(8,128)(2,1)}, u32[]{:S(2)}) copy-start(bf16[9,128]{1,0:T(8,128)(2,1)} %param.28) | copy-start | bytes 6916
  249.2 9.7 %copy-start.12 = (bf16[128,1024]{1,0:T(8,128)(2,1)S(1)}, bf16[128,1024]{1,0:T(8,128)(2,1)}, u32[]{:S(2)}) copy-start(bf16[128,1024]{1,0:T(8,128)(2,1)} %param.25) | copy-start | bytes 786436
  249.2 95.0 %all-gather.10.cloned.1.call-start = ((), (), s32[]{:S(2)}) async-start(), calls=%async_computation.4 | async-start | bytes 2433024 | tf_op jit(solution)/shard_map/all_gather | solution.py:197
  249.3 3.9 %collective-permute-start = (bf16[128,1024]{1,0:T(8,128)(2,1)}, bf16[128,1024]{1,0:T(8,128)(2,1)S(1)}, u32[]{:S(2)}, u32[]{:S(2)}) collective-permute-start(bf16[128,1024]{1,0:T(8,128)(2,1)} %param.25), channel_id=1, source_target_pairs={{0,64},{64,128},{128,192},{192,256},{256,320},{320,384},{384,448},... | collective-permute-start | bytes 786440 | tf_op jit(solution)/shard_map/ppermute | solution.py:22
  249.5 6.6 %collective-permute-start.1 = (bf16[128,1024]{1,0:T(8,128)(2,1)}, bf16[128,1024]{1,0:T(8,128)(2,1)S(1)}, u32[]{:S(2)}, u32[]{:S(2)}) collective-permute-start(bf16[128,1024]{1,0:T(8,128)(2,1)} %param.25), channel_id=1, source_target_pairs={{0,448},{64,0},{128,64},{192,128},{256,192},{320,256},{384,320},{4... | collective-permute-start | bytes 786440 | tf_op jit(solution)/shard_map/ppermute | solution.py:29
  253.2 7.2 %collective-permute-start.2 = (bf16[128,1024]{1,0:T(8,128)(2,1)S(1)}, bf16[128,1024]{1,0:T(8,128)(2,1)}, u32[]{:S(2)}, u32[]{:S(2)}) collective-permute-start(bf16[128,1024]{1,0:T(8,128)(2,1)S(1)} %collective-permute-done), channel_id=1, source_target_pairs={{0,64},{64,128},{128,192},{192,256},{256,320},{320,384},{384,448},... | collective-permute-start | bytes 786440 | tf_op jit(solution)/shard_map/ppermute | solution.py:22
  256.2 6.7 %collective-permute-start.3 = (bf16[128,1024]{1,0:T(8,128)(2,1)S(1)}, bf16[128,1024]{1,0:T(8,128)(2,1)}, u32[]{:S(2)}, u32[]{:S(2)}) collective-permute-start(bf16[128,1024]{1,0:T(8,128)(2,1)S(1)} %collective-permute-done.1), channel_id=1, source_target_pairs={{0,448},{64,0},{128,64},{192,128},{256,192},{320,256},{384,320},{4... | collective-permute-start | bytes 786440 | tf_op jit(solution)/shard_map/ppermute | solution.py:29
  260.3 6.7 %collective-permute-start.4 = (bf16[128,1024]{1,0:T(8,128)(2,1)}, bf16[128,1024]{1,0:T(8,128)(2,1)S(1)}, u32[]{:S(2)}, u32[]{:S(2)}) collective-permute-start(bf16[128,1024]{1,0:T(8,128)(2,1)} %collective-permute-done.2), channel_id=1, source_target_pairs={{0,64},{64,128},{128,192},{192,256},{256,320},{320,384},{384,448},... | collective-permute-start | bytes 786440 | tf_op jit(solution)/shard_map/ppermute | solution.py:22
  262.9 7.0 %collective-permute-start.5 = (bf16[128,1024]{1,0:T(8,128)(2,1)}, bf16[128,1024]{1,0:T(8,128)(2,1)S(1)}, u32[]{:S(2)}, u32[]{:S(2)}) collective-permute-start(bf16[128,1024]{1,0:T(8,128)(2,1)} %collective-permute-done.3), channel_id=1, source_target_pairs={{0,448},{64,0},{128,64},{192,128},{256,192},{320,256},{384,320},{4... | collective-permute-start | bytes 786440 | tf_op jit(solution)/shard_map/ppermute | solution.py:29
  267.0 7.5 %collective-permute-start.6 = (bf16[128,1024]{1,0:T(8,128)(2,1)S(1)}, bf16[128,1024]{1,0:T(8,128)(2,1)S(1)}, u32[]{:S(2)}, u32[]{:S(2)}) collective-permute-start(bf16[128,1024]{1,0:T(8,128)(2,1)S(1)} %collective-permute-done.4), channel_id=1, source_target_pairs={{0,64},{64,128},{128,192},{192,256},{256,320},{320,384},{384,448},... | collective-permute-start | bytes 786440 | tf_op jit(solution)/shard_map/ppermute | solution.py:22
  297.1 3.6 %copy-start.15 = (f32[1024]{0:T(1024)S(1)}, f32[1024]{0:T(1024)}, u32[]{:S(2)}) copy-start(f32[1024]{0:T(1024)} %param.26) | copy-start | bytes 12292
  313.1 33.6 %all-to-all-start.1 = ((bf16[8,128,128]{2,1,0:T(8,128)(2,1)}), bf16[8,128,128]{2,1,0:T(8,128)(2,1)}, u32[]{:S(2)}, u32[]{:S(2)}) async-start(bf16[8,128,128]{2,1,0:T(8,128)(2,1)} %bitcast.18), calls=%async_computation.1 | async-start | bytes 524288 | tf_op jit(solution)/shard_map/all_to_all | solution.py:90
  321.1 2.8 copy-start.10
  344.2 6.4 %copy-start.1 = (bf16[1024,1,384]{2,0,1:T(8,128)(2,1)S(1)}, bf16[1024,1,384]{2,0,1:T(8,128)(2,1)}, u32[]{:S(2)}) copy-start(bf16[1024,1,384]{2,0,1:T(8,128)(2,1)} %param.24) | copy-start | bytes 2359300
  (18 other events, 31.1 us)
Sparse Core Ops, SparseCore 0:
  192.2 32.6 all-gather.5
  249.3 35.2 all-gather.7
  311.3 32.8 all-gather.9
